TPU v7x, 512 devices: a whole 4x8x8 slice. The times are simulated.
512 devices in a mesh: space: 32 (over x, y_hi, core), tm: 16 (over z, y_lo).
Axes of the slice: x: 4, y: 8 (y_hi: 4, y_lo: 2; y = y_hi * 2 + y_lo), z: 8, core: 2. Of those that a mesh axis runs over, the one named last changes fastest.
Arguments:
- field: float32 [256, 32768], P('tm', 'space'), may hold values from -6 to 6
- momentum: float32 [256, 32768], P('tm', 'space'), may hold values from -6 to 6
- solution: float32 [256, 32768], P('tm', 'space'), may hold values from -6 to 6
- tiles: float32 [256, 6, 128, 128], P('space'), may hold values from -1 to 2
- columns: int32 [256, 6], P('space'), may hold values from 0 to 255, as said below
- neighbours: int32 [3, 32768], P(None, 'space'), may hold values from 0 to 32767, as said below
Outputs:
- field_out: float32 [256, 32768], P('tm', 'space')
- momentum_out: float32 [256, 32768], P('tm', 'space')
- fermion_force: float32 [256, 32768], P('tm', 'space')
Inputs may be any that keep to these rules, and one draw needn't show every extreme that they name: Row r lists 6 different tile columns, the first of them r itself; the others lie outside the run of 8 tile rows that holds r (runs r // 8), and the rows of one run name at most 2 columns of any other run, exactly 2 for some run. The neighbour relation is symmetric, each site has three different neighbours, and each neighbour lies in the site's own run of 128 labels or in the run just before or after it, cyclically over the flake.
All inputs are finite; a program needn't handle non-finite values.
Results may differ from a plain program's by a relative error of at most 0.00014.
Values sent between devices are 32-bit elements; how exact they have to be, the bound alone decides.
No kernel may reach another device: no remote copies, remote signals or barrier semaphores. Data moves between devices by JAX's collectives and lax.ppermute only.
A program may use at most 64 MiB of HBM per device.

v0:
```python
import jax
import jax.numpy as jnp
from jax import lax
from jax.sharding import PartitionSpec as P

TILE = 128
step_size = 0.5
hop_kappa = 0.5
coupling = 0.25


def with_halo(block, sides, width):
    for axis, dim in sides:
        count = lax.axis_size(axis)
        forward = [(i, i + 1) for i in range(count - 1)]
        forward.append((count - 1, 0))
        backward = [(target, source) for source, target in forward]
        low = lax.ppermute(
            lax.slice_in_dim(block, block.shape[dim] - width, None, axis=dim), axis, forward
        )
        high = lax.ppermute(lax.slice_in_dim(block, 0, width, axis=dim), axis, backward)
        block = jnp.concatenate([low, block, high], axis=dim)
    return block


def from_behind(value, axis, steps):
    count = lax.axis_size(axis)
    pairs = [(source, (source + steps) % count) for source in range(count)]
    return lax.ppermute(value, axis, pairs)


def body(field, momentum, solution, tiles, columns, neighbours):
    slices = field.shape[0]
    tile_rows = tiles.shape[0]
    kept = tiles.shape[1]
    site_count = field.shape[1]
    cols_flat = columns.reshape(-1)
    space_count = lax.axis_size("space")

    def coulomb(values):
        gathered = lax.all_gather(values, "space", axis=1, tiled=True)
        blocks = gathered.reshape(slices, -1, TILE)
        picked = jnp.take(blocks, cols_flat, axis=1).reshape(slices, tile_rows, kept, TILE)
        mixed = jnp.einsum("rkij,trkj->tri", tiles, picked, precision=lax.Precision.HIGHEST)
        return mixed.reshape(slices, site_count)

    moment = momentum - 0.5 * step_size * coulomb(field)
    field_one = field + step_size * moment
    moment = moment - step_size * coulomb(field_one)
    field_two = field_one + step_size * moment
    moment = moment - 0.5 * step_size * coulomb(field_two)
    total_sites = site_count * space_count
    first_site = lax.axis_index("space") * site_count
    lookup = (neighbours - first_site + TILE) % total_sites
    parity_sign = jnp.where(lax.axis_index("tm") == 0, -1.0, 1.0).astype(jnp.float32)
    widened = with_halo(solution, (("space", 1),), TILE)
    beside = jnp.take(widened, lookup.reshape(-1), axis=1).reshape(solution.shape[0], 3, site_count)
    hopped = solution + hop_kappa * (beside[:, 0] + beside[:, 1] + beside[:, 2])
    arrived = from_behind(hopped[-1:], "tm", 1)
    earlier = jnp.concatenate([parity_sign * arrived, hopped[:-1]], axis=0)
    link_factor = jnp.exp(coupling * field_two)
    shifted = solution - link_factor * earlier
    force = 2.0 * coupling * shifted * link_factor * earlier
    return (field_two, moment, force)


def solution(mesh):
    in_specs = (
        P("tm", "space"),
        P("tm", "space"),
        P("tm", "space"),
        P("space", None, None, None),
        P("space", None),
        P(None, "space"),
    )
    out_specs = (P("tm", "space"), P("tm", "space"), P("tm", "space"))
    return jax.shard_map(body, mesh=mesh, in_specs=in_specs, out_specs=out_specs, check_vma=False)
```

profile of v0, /device:TPU:1, one launch (start us, length us, event | category | flops | bytes accessed | tf_op | source)
XLA Modules:
  0.0 224.8 jit_solution(11539361856187728963)
XLA Ops:
  7.2 0.0 copy-start
  7.2 0.0 all-gather.4.cloned.1.call-start
  7.2 0.7 all-gather.4.cloned.1.call-update
  7.9 0.0 all-gather.6.cloned.1.call-start
  8.0 0.9 reshape.89
  8.9 67.8 %all-gather.4.cloned.1.call-done = f32[16,32768]{1,0:T(8,128)} async-done(((f32[16,1024]{1,0:T(8,128)}), f32[16,32768]{1,0:T(8,128)}) %all-gather.4.cloned.1.call-update) | async-done | bytes 2097168 | tf_op jit(solution)/shard_map/all_gather | solution.py:41
  76.7 3.1 %copy_bitcast_fusion.2 = f32[16,256,128]{2,0,1:T(8,128)} fusion(f32[16,32768]{1,0:T(8,128)} %all-gather.4.cloned.1.call-done), kind=kLoop, calls=%fused_computation.6 | loop fusion | bytes 4194304 | tf_op jit(solution)/shard_map/reshape | solution.py:42
  79.8 2.2 gather_fusion.1
  82.0 0.0 copy-start.8
  82.0 0.0 copy-start.14
  82.0 0.1 broadcast_select_fusion.2
  82.1 0.0 copy-start.4
  82.1 0.0 copy-start.15
  82.2 2.7 %fusion.5 = f32[8,2,8,128]{3,2,1,0:T(8,128)S(1)} fusion(f32[16,8,6,128]{3,0,2,1:T(8,128)S(1)} %bitcast.95, f32[8,6,128,128]{3,2,1,0:T(8,128)S(1)} %copy-done), kind=kOutput, calls=%fused_computation.15 | convolution fusion | flops 151011328 | bytes 3604480 | tf_op jit(solution)/shard_map/rkij,trkj->tri/dot_general | solution.py:44
  84.9 0.6 copy-done.1
  85.5 0.6 multiply_add_fusion.1
  86.2 0.0 all-gather.6.cloned.1.call-update
  86.2 0.0 all-gather.8.cloned.1.call-start
  86.3 3.0 %collective-permute-start = (f32[16,128]{1,0:T(8,128)S(1)}, f32[16,128]{1,0:T(8,128)S(1)}, u32[]{:S(2)}, u32[]{:S(2)}) collective-permute-start(f32[16,128]{1,0:T(8,128)S(1)} %get-tuple-element.8), channel_id=1, source_target_pairs={{0,16},{16,32},{32,48},{48,64},{64,80},{80,96},{96,112},{112,128},... | collective-permute-start | bytes 24584 | tf_op jit(solution)/shard_map/ppermute | solution.py:18
  89.3 1.9 collective-permute-start.1
  91.3 4.0 %collective-permute-done.1 = f32[16,128]{1,0:T(8,128)S(1)} collective-permute-done((f32[16,128]{1,0:T(8,128)S(1)}, f32[16,128]{1,0:T(8,128)S(1)}, u32[]{:S(2)}, u32[]{:S(2)}) %collective-permute-start.1) | collective-permute-done | bytes 8224 | tf_op jit(solution)/shard_map/ppermute | solution.py:21
  95.3 1.1 copy.39
  96.4 12.0 %gather_fusion = f32[3072,16]{1,0:T(8,128)} fusion(f32[16,1280]{0,1:T(8,128)} %copy.39, s32[3072]{0:T(1024)S(1)} %broadcast_clamp_fusion), kind=kCustom, calls=%fused_computation.3 | custom fusion | bytes 405504 | tf_op jit(solution)/shard_map/jit(_take)/gather | solution.py:57
  108.4 1.8 copy.40
  110.3 0.0 copy-start.12
  110.3 0.6 copy-done.12
  110.9 2.7 %collective-permute-start.2 = (f32[1,1024]{1,0:T(1,128)S(1)}, f32[1,1024]{1,0:T(1,128)S(1)}, u32[]{:S(2)}, u32[]{:S(2)}) collective-permute-start(f32[1,1024]{1,0:T(1,128)S(1)} %slice.39), channel_id=1, source_target_pairs={{0,1},{1,2},{2,3},{3,4},{4,5},{5,6},{6,7},{7,8},{8,9},{9,10},{10,1... | collective-permute-start | bytes 12296 | tf_op jit(solution)/shard_map/ppermute | solution.py:29
  113.6 4.4 %collective-permute-done.2 = f32[1,1024]{1,0:T(1,128)S(1)} collective-permute-done((f32[1,1024]{1,0:T(1,128)S(1)}, f32[1,1024]{1,0:T(1,128)S(1)}, u32[]{:S(2)}, u32[]{:S(2)}) %collective-permute-start.2) | collective-permute-done | bytes 4128 | tf_op jit(solution)/shard_map/ppermute | solution.py:29
  118.0 25.4 %all-gather.6.cloned.1.call-done = f32[16,32768]{1,0:T(8,128)} async-done(((f32[16,1024]{1,0:T(8,128)}), f32[16,32768]{1,0:T(8,128)}) %all-gather.6.cloned.1.call-update) | async-done | bytes 2097168 | tf_op jit(solution)/shard_map/all_gather | solution.py:41
  143.4 3.1 %copy_bitcast_fusion.1 = f32[16,256,128]{2,0,1:T(8,128)} fusion(f32[16,32768]{1,0:T(8,128)} %all-gather.6.cloned.1.call-done), kind=kLoop, calls=%fused_computation.5 | loop fusion | bytes 4194304 | tf_op jit(solution)/shard_map/reshape | solution.py:42
  146.5 2.2 gather_fusion.2
  148.6 0.0 copy-start.5
  148.7 0.0 copy-start.9
  148.7 0.0 copy-start.11
  148.7 0.0 copy-start.13
  148.7 0.1 broadcast_select_fusion.1
  148.8 2.7 %fusion.3 = f32[8,2,8,128]{3,2,1,0:T(8,128)S(1)} fusion(f32[16,8,6,128]{3,0,2,1:T(8,128)S(1)} %bitcast.96, f32[8,6,128,128]{3,2,1,0:T(8,128)S(1)} %copy-done), kind=kOutput, calls=%fused_computation.12 | convolution fusion | flops 151011328 | bytes 3604480 | tf_op jit(solution)/shard_map/rkij,trkj->tri/dot_general | solution.py:44
  151.5 0.0 copy-done.2
  151.6 0.7 multiply_multiply_fusion
  152.3 0.0 all-gather.8.cloned.1.call-update
  152.3 57.2 %all-gather.8.cloned.1.call-done = f32[16,32768]{1,0:T(8,128)} async-done(((f32[16,1024]{1,0:T(8,128)}), f32[16,32768]{1,0:T(8,128)}) %all-gather.8.cloned.1.call-update) | async-done | bytes 2097168 | tf_op jit(solution)/shard_map/all_gather | solution.py:41
  209.5 3.1 %copy_bitcast_fusion = f32[16,256,128]{2,0,1:T(8,128)} fusion(f32[16,32768]{1,0:T(8,128)} %all-gather.8.cloned.1.call-done), kind=kLoop, calls=%fused_computation.4 | loop fusion | bytes 4194304 | tf_op jit(solution)/shard_map/reshape | solution.py:42
  212.6 2.2 gather_fusion.3
  214.8 0.0 copy-start.10
  214.8 0.1 broadcast_select_fusion
  214.9 2.7 %fusion.1 = f32[8,2,8,128]{3,2,1,0:T(8,128)S(1)} fusion(f32[16,8,6,128]{3,0,2,1:T(8,128)S(1)} %bitcast.94, f32[8,6,128,128]{3,2,1,0:T(8,128)S(1)} %copy-done), kind=kOutput, calls=%fused_computation.9 | convolution fusion | flops 151011328 | bytes 3604480 | tf_op jit(solution)/shard_map/rkij,trkj->tri/dot_general | solution.py:44
  217.6 0.0 copy-done.7
  217.7 0.6 bitcast_subtract_fusion
  (31 shorter events, 0.2 us)
Async XLA Ops:
  7.2 75.0 %copy-start = (f32[8,6,128,128]{3,2,1,0:T(8,128)S(1)}, f32[8,6,128,128]{3,2,1,0:T(8,128)}, u32[]{:S(2)}) copy-start(f32[8,6,128,128]{3,2,1,0:T(8,128)} %param.11) | copy-start | bytes 9437188
  7.2 69.6 %all-gather.4.cloned.1.call-start = ((), (), s32[]{:S(2)}) async-start(), calls=%async_computation | async-start | bytes 2162688 | tf_op jit(solution)/shard_map/all_gather | solution.py:41
  7.9 135.5 %all-gather.6.cloned.1.call-start = ((), (), s32[]{:S(2)}) async-start(), calls=%async_computation.1 | async-start | bytes 2162688 | tf_op jit(solution)/shard_map/all_gather | solution.py:41
  82.0 3.6 %copy-start.8 = (f32[16,1024]{1,0:T(8,128)S(1)}, f32[16,1024]{1,0:T(8,128)}, u32[]{:S(2)}) copy-start(f32[16,1024]{1,0:T(8,128)} %param.9) | copy-start | bytes 196612
  82.0 3.6 %copy-start.14 = (f32[16,1024]{1,0:T(8,128)S(1)}, f32[16,1024]{1,0:T(8,128)}, u32[]{:S(2)}) copy-start(f32[16,1024]{1,0:T(8,128)} %param.8) | copy-start | bytes 196612
  82.1 4.1 %copy-start.4 = (f32[16,1024]{1,0:T(8,128)S(1)}, f32[16,1024]{1,0:T(8,128)}, u32[]{:S(2)}) copy-start(f32[16,1024]{1,0:T(8,128)} %param.10) | copy-start | bytes 196612
  82.1 9.1 %copy-start.15 = (s32[3,1024]{1,0:T(4,128)S(1)}, s32[3,1024]{1,0:T(4,128)}, u32[]{:S(2)}) copy-start(s32[3,1024]{1,0:T(4,128)} %param.13) | copy-start | bytes 36868
  84.9 0.6 copy-start.1
  86.2 123.3 %all-gather.8.cloned.1.call-start = ((), (), s32[]{:S(2)}) async-start(), calls=%async_computation.2 | async-start | bytes 2162688 | tf_op jit(solution)/shard_map/all_gather | solution.py:41
  86.3 5.0 %collective-permute-start = (f32[16,128]{1,0:T(8,128)S(1)}, f32[16,128]{1,0:T(8,128)S(1)}, u32[]{:S(2)}, u32[]{:S(2)}) collective-permute-start(f32[16,128]{1,0:T(8,128)S(1)} %get-tuple-element.8), channel_id=1, source_target_pairs={{0,16},{16,32},{32,48},{48,64},{64,80},{80,96},{96,112},{112,128},... | collective-permute-start | bytes 24584 | tf_op jit(solution)/shard_map/ppermute | solution.py:18
  89.3 6.1 %collective-permute-start.1 = (f32[16,128]{1,0:T(8,128)S(1)}, f32[16,128]{1,0:T(8,128)S(1)}, u32[]{:S(2)}, u32[]{:S(2)}) collective-permute-start(f32[16,128]{1,0:T(8,128)S(1)} %get-tuple-element.9), channel_id=1, source_target_pairs={{16,0},{32,16},{48,32},{64,48},{80,64},{96,80},{112,96},{128,112},... | collective-permute-start | bytes 24584 | tf_op jit(solution)/shard_map/ppermute | solution.py:21
  110.3 0.6 copy-start.12
  110.9 7.0 %collective-permute-start.2 = (f32[1,1024]{1,0:T(1,128)S(1)}, f32[1,1024]{1,0:T(1,128)S(1)}, u32[]{:S(2)}, u32[]{:S(2)}) collective-permute-start(f32[1,1024]{1,0:T(1,128)S(1)} %slice.39), channel_id=1, source_target_pairs={{0,1},{1,2},{2,3},{3,4},{4,5},{5,6},{6,7},{7,8},{8,9},{9,10},{10,1... | collective-permute-start | bytes 12296 | tf_op jit(solution)/shard_map/ppermute | solution.py:29
  148.6 2.9 %copy-start.2 = (f32[8,2,8,128]{3,2,1,0:T(8,128)S(1)}, f32[8,2,8,128]{3,2,1,0:T(8,128)}, u32[]{:S(2)}) copy-start(f32[8,2,8,128]{3,2,1,0:T(8,128)} %copy-done.1) | copy-start | bytes 196612
  148.6 2.9 %copy-start.5 = (f32[16,1024]{1,0:T(8,128)S(1)}, f32[16,1024]{1,0:T(8,128)}, u32[]{:S(2)}) copy-start(f32[16,1024]{1,0:T(8,128)} %param.10) | copy-start | bytes 196612
  148.7 2.9 %copy-start.9 = (f32[16,1024]{1,0:T(8,128)S(1)}, f32[16,1024]{1,0:T(8,128)}, u32[]{:S(2)}) copy-start(f32[16,1024]{1,0:T(8,128)} %param.9) | copy-start | bytes 196612
  148.7 2.9 %copy-start.11 = (f32[16,1024]{1,0:T(8,128)S(1)}, f32[16,1024]{1,0:T(8,128)}, u32[]{:S(2)}) copy-start(f32[16,1024]{1,0:T(8,128)} %multiply_add_fusion.1) | copy-start | bytes 196612
  148.7 2.9 %copy-start.13 = (f32[16,1024]{1,0:T(8,128)S(1)}, f32[16,1024]{1,0:T(8,128)}, u32[]{:S(2)}) copy-start(f32[16,1024]{1,0:T(8,128)} %copy-done.12) | copy-start | bytes 196612
  151.5 0.8 copy-start.6
  214.7 2.9 %copy-start.3 = (f32[8,2,8,128]{3,2,1,0:T(8,128)S(1)}, f32[8,2,8,128]{3,2,1,0:T(8,128)}, u32[]{:S(2)}) copy-start(f32[8,2,8,128]{3,2,1,0:T(8,128)} %copy-done.1) | copy-start | bytes 196612
  214.8 2.9 %copy-start.7 = (f32[8,2,8,128]{3,2,1,0:T(8,128)S(1)}, f32[8,2,8,128]{3,2,1,0:T(8,128)}, u32[]{:S(2)}) copy-start(f32[8,2,8,128]{3,2,1,0:T(8,128)} %copy-done.6) | copy-start | bytes 196612
  214.8 2.9 %copy-start.10 = (f32[16,1024]{1,0:T(8,128)S(1)}, f32[16,1024]{1,0:T(8,128)}, u32[]{:S(2)}) copy-start(f32[16,1024]{1,0:T(8,128)} %param.9) | copy-start | bytes 196612
Sparse Core Ops, SparseCore 0:
  11.2 65.4 all-gather.3
  86.3 57.0 all-gather.5
  152.5 57.0 all-gather.7
where the time goes:
time: 225 us
  waiting for transfers between devices  160 us (71%)
  local copies, waits for them, and re-layouts  32.9 us (15%)
  between operations  14.1 us (6%)
  matrix products  8.19 us (4%)
  starting transfers between devices  7.67 us (3%)
  other arithmetic  2.47 us (1%)
    all_gather x3, waiting for transfers between devices, coulomb(): gathered = lax.all_gather(values, 'space', axis=1, tiled=True)  150 us
    gather x2, local copies, waits for them, and re-layouts, body(): jnp.take(widened, lookup.reshape(-1), axis=1)  13.8 us
    reshape x3, local copies, waits for them, and re-layouts, coulomb(): blocks = gathered.reshape(slices, -1, TILE)  9.16 us
    dot_general x3, matrix products, coulomb(): jnp.einsum('rkij,trkj->tri', tiles, picked, precision=lax.Precision.HIGHEST)  8.19 us
    gather x3, local copies, waits for them, and re-layouts, coulomb(): jnp.take(blocks, cols_flat, axis=1).reshape(slices, tile_rows, kept, TILE)  6.51 us
  transfers between devices with their start and end apart: 6, of which 5 were waited for; matrix products, arithmetic and copies ran while one was open for 7% of the time, Pallas kernels for 0%

commit v1 on v0

--- a/solution.py
+++ b/solution.py
@@ -38,7 +38,10 @@
     space_count = lax.axis_size("space")
 
     def coulomb(values):
-        gathered = lax.all_gather(values, "space", axis=1, tiled=True)
+        size = lax.axis_size("space")
+        parts = jnp.stack([values for _ in range(size)])
+        parts = lax.all_to_all(parts, "space", split_axis=0, concat_axis=0)
+        gathered = jnp.concatenate(parts, axis=1)
         blocks = gathered.reshape(slices, -1, TILE)
         picked = jnp.take(blocks, cols_flat, axis=1).reshape(slices, tile_rows, kept, TILE)
         mixed = jnp.einsum("rkij,trkj->tri", tiles, picked, precision=lax.Precision.HIGHEST)

time: 225 us -> 253 us (1.12)
  waiting for transfers between devices: 160 us -> 96.2 us
  blocking collectives: 0 us -> 59.8 us
  local copies, waits for them, and re-layouts: 32.9 us -> 59.2 us
  starting transfers between devices: 7.67 us -> 26.3 us
  between operations: 14.1 us -> 1.02 us
    all_gather x3 -> x0, waiting for transfers between devices: 150 us -> none  [coulomb(): gathered = lax.all_gather(values, 'space', axis=1, tiled=True)]
    all_to_all x0 -> x1, blocking collectives: none -> 59.8 us  [coulomb(): parts = lax.all_to_all(parts, 'space', split_axis=0, concat_axis=0)]
    all_to_all x0 -> x2, waiting for transfers between devices: none -> 50.9 us  [coulomb(): parts = lax.all_to_all(parts, 'space', split_axis=0, concat_axis=0)]
    ppermute x1, waiting for transfers between devices: 0.01 us -> 37.5 us  [with_halo(): lax.ppermute(lax.slice_in_dim(block, block.shape[dim] - width, None, axis...]
    another operation x0 -> x9, local copies, waits for them, and re-layouts: none -> 24.9 us  [the longest x6 20.5 us: coulomb(): blocks = gathered.reshape(slices, -1, TILE)]
    all_to_all x0 -> x2, starting transfers between devices: none -> 17.9 us  [coulomb(): parts = lax.all_to_all(parts, 'space', split_axis=0, concat_axis=0)]
  transfers between devices with their start and end apart: 6 -> 5, of which waited for: 5 -> 4; matrix products, arithmetic and copies ran while one was open for 7% -> 6% of each run, Pallas kernels for 0% -> 0%
where the time goes in v1:
time: 253 us
  waiting for transfers between devices  96.2 us (38%)
  blocking collectives  59.8 us (24%)
  local copies, waits for them, and re-layouts  59.2 us (23%)
  starting transfers between devices  26.3 us (10%)
  matrix products  8.19 us (3%)
    all_to_all x1, blocking collectives, coulomb(): parts = lax.all_to_all(parts, 'space', split_axis=0, concat_axis=0)  59.8 us
    all_to_all x2, waiting for transfers between devices, coulomb(): parts = lax.all_to_all(parts, 'space', split_axis=0, concat_axis=0)  50.9 us
    ppermute x1, waiting for transfers between devices, with_halo(): lax.ppermute(lax.slice_in_dim(block, block.shape[dim] - width, None, axis...  37.5 us
    another operation x6, local copies, waits for them, and re-layouts, coulomb(): blocks = gathered.reshape(slices, -1, TILE)  20.5 us
    all_to_all x2, starting transfers between devices, coulomb(): parts = lax.all_to_all(parts, 'space', split_axis=0, concat_axis=0)  17.9 us
    gather x2, local copies, waits for them, and re-layouts, body(): jnp.take(widened, lookup.reshape(-1), axis=1)  13.8 us
    reshape x3, local copies, waits for them, and re-layouts, coulomb(): gathered = jnp.concatenate(parts, axis=1)  10.8 us
    dot_general x3, matrix products, coulomb(): jnp.einsum('rkij,trkj->tri', tiles, picked, precision=lax.Precision.HIGHEST)  8.19 us
  transfers between devices with their start and end apart: 5, of which 4 were waited for; matrix products, arithmetic and copies ran while one was open for 6% of the time, Pallas kernels for 0%

profile of v1, /device:TPU:1, one launch (start us, length us, event | category | flops | bytes accessed | tf_op | source)
XLA Modules:
  0.0 252.6 jit_solution(16299675782434079316)
XLA Ops:
  0.6 0.0 copy-start
  0.6 2.6 %stack.6 = f32[32,16,1024]{2,1,0:T(8,128)} broadcast(f32[16,1024]{1,0:T(8,128)} %param.8), dimensions={1,2} | broadcast | bytes 2162688 | tf_op jit(solution)/shard_map/stack | solution.py:42
  3.2 11.4 %all-to-all-start = ((f32[32,16,1024]{2,1,0:T(8,128)}), f32[32,16,1024]{2,1,0:T(8,128)}, u32[]{:S(2)}, u32[]{:S(2)}) async-start(f32[32,16,1024]{2,1,0:T(8,128)} %stack.6), calls=%async_computation | async-start | bytes 4194304 | tf_op jit(solution)/shard_map/all_to_all | solution.py:43
  14.6 0.1 reshape.95
  14.7 50.9 %all-to-all-done = f32[32,16,1024]{2,1,0:T(8,128)} async-done(((f32[32,16,1024]{2,1,0:T(8,128)}), f32[32,16,1024]{2,1,0:T(8,128)}, u32[]{:S(2)}, u32[]{:S(2)}) %all-to-all-start) | async-done | bytes 2097184 | tf_op jit(solution)/shard_map/all_to_all | solution.py:43
  65.7 4.1 %copy.23 = f32[16,32,1024]{2,1,0:T(8,128)} copy(f32[16,32,1024]{2,0,1:T(8,128)} %bitcast) | data formatting | bytes 4194304 | tf_op jit(solution)/shard_map/reshape | solution.py:44
  69.8 2.7 %reshape_reshape.9 = f32[16,256,128]{2,1,0:T(8,128)} reshape(f32[16,32,1024]{2,1,0:T(8,128)} %copy.23) | data formatting | bytes 4194304 | tf_op jit(solution)/shard_map/reshape;reshape | solution.py:45
  72.5 4.1 %copy.24 = f32[16,256,128]{2,0,1:T(8,128)} copy(f32[16,256,128]{2,1,0:T(8,128)} %reshape_reshape.9) | data formatting | bytes 4194304 | tf_op jit(solution)/shard_map/reshape;reshape | solution.py:45
  76.6 2.2 gather_fusion.1
  78.8 0.0 copy-start.8
  78.8 0.0 copy-start.15
  78.8 0.1 broadcast_select_fusion.2
  79.0 2.7 %fusion.5 = f32[8,2,8,128]{3,2,1,0:T(8,128)S(1)} fusion(f32[16,8,6,128]{3,0,2,1:T(8,128)S(1)} %bitcast.84, f32[8,6,128,128]{3,2,1,0:T(8,128)S(1)} %copy-done), kind=kOutput, calls=%fused_computation.12 | convolution fusion | flops 151011328 | bytes 3604480 | tf_op jit(solution)/shard_map/rkij,trkj->tri/dot_general | solution.py:47
  81.7 0.6 copy-done.1
  82.4 0.0 copy-start.11
  82.4 0.6 copy-done.11
  83.0 1.6 stack.7
  84.6 6.5 %all-to-all-start.1 = ((f32[32,16,1024]{2,1,0:T(8,128)}), f32[32,16,1024]{2,1,0:T(8,128)}, u32[]{:S(2)}, u32[]{:S(2)}) async-start(f32[32,16,1024]{2,1,0:T(8,128)} %stack.7), calls=%async_computation.1 | async-start | bytes 4194304 | tf_op jit(solution)/shard_map/all_to_all | solution.py:43
  91.1 4.4 %collective-permute-start = (f32[16,128]{1,0:T(8,128)S(1)}, f32[16,128]{1,0:T(8,128)S(1)}, u32[]{:S(2)}, u32[]{:S(2)}) collective-permute-start(f32[16,128]{1,0:T(8,128)S(1)} %get-tuple-element.8), channel_id=1, source_target_pairs={{0,16},{16,32},{32,48},{48,64},{64,80},{80,96},{96,112},{112,128},... | collective-permute-start | bytes 24584 | tf_op jit(solution)/shard_map/ppermute | solution.py:18
  95.5 1.9 collective-permute-start.1
  97.6 37.5 %collective-permute-done = f32[16,128]{1,0:T(8,128)S(1)} collective-permute-done((f32[16,128]{1,0:T(8,128)S(1)}, f32[16,128]{1,0:T(8,128)S(1)}, u32[]{:S(2)}, u32[]{:S(2)}) %collective-permute-start) | collective-permute-done | bytes 8224 | tf_op jit(solution)/shard_map/ppermute | solution.py:18
  135.1 3.4 %collective-permute-done.1 = f32[16,128]{1,0:T(8,128)S(1)} collective-permute-done((f32[16,128]{1,0:T(8,128)S(1)}, f32[16,128]{1,0:T(8,128)S(1)}, u32[]{:S(2)}, u32[]{:S(2)}) %collective-permute-start.1) | collective-permute-done | bytes 8224 | tf_op jit(solution)/shard_map/ppermute | solution.py:21
  138.5 1.1 copy.32
  139.6 12.0 %gather_fusion = f32[3072,16]{1,0:T(8,128)} fusion(f32[16,1280]{0,1:T(8,128)} %copy.32, s32[3072]{0:T(1024)S(1)} %broadcast_clamp_fusion), kind=kCustom, calls=%fused_computation.3 | custom fusion | bytes 405504 | tf_op jit(solution)/shard_map/jit(_take)/gather | solution.py:60
  151.6 1.8 copy.33
  153.5 0.6 copy-done.13
  154.1 2.1 collective-permute-start.2
  156.2 4.3 %collective-permute-done.2 = f32[1,1024]{1,0:T(1,128)S(1)} collective-permute-done((f32[1,1024]{1,0:T(1,128)S(1)}, f32[1,1024]{1,0:T(1,128)S(1)}, u32[]{:S(2)}, u32[]{:S(2)}) %collective-permute-start.2) | collective-permute-done | bytes 4128 | tf_op jit(solution)/shard_map/ppermute | solution.py:29
  160.6 4.1 %copy.26 = f32[16,32,1024]{2,1,0:T(8,128)} copy(f32[16,32,1024]{2,0,1:T(8,128)} %bitcast.6) | data formatting | bytes 4194304 | tf_op jit(solution)/shard_map/reshape | solution.py:44
  164.7 2.7 %reshape_reshape.10 = f32[16,256,128]{2,1,0:T(8,128)} reshape(f32[16,32,1024]{2,1,0:T(8,128)} %copy.26) | data formatting | bytes 4194304 | tf_op jit(solution)/shard_map/reshape;reshape | solution.py:45
  167.4 4.1 %copy.27 = f32[16,256,128]{2,0,1:T(8,128)} copy(f32[16,256,128]{2,1,0:T(8,128)} %reshape_reshape.10) | data formatting | bytes 4194304 | tf_op jit(solution)/shard_map/reshape;reshape | solution.py:45
  171.5 2.2 gather_fusion.2
  173.7 0.0 copy-start.5
  173.8 0.0 copy-start.14
  173.8 0.1 broadcast_select_fusion.1
  173.9 2.7 %fusion.3 = f32[8,2,8,128]{3,2,1,0:T(8,128)S(1)} fusion(f32[16,8,6,128]{3,0,2,1:T(8,128)S(1)} %bitcast.85, f32[8,6,128,128]{3,2,1,0:T(8,128)S(1)} %copy-done), kind=kOutput, calls=%fused_computation.9 | convolution fusion | flops 151011328 | bytes 3604480 | tf_op jit(solution)/shard_map/rkij,trkj->tri/dot_general | solution.py:47
  176.6 0.0 copy-done.2
  176.7 0.7 multiply_multiply_fusion
  177.4 0.2 stack.8
  177.6 59.8 %all_to_all.15 = f32[32,16,1024]{2,1,0:T(8,128)S(1)} all-to-all(f32[32,16,1024]{2,1,0:T(8,128)S(1)} %stack.8), channel_id=1, replica_groups=mesh['space'=32,'tm'=16] {'space'}, dimensions={0} | all-to-all | bytes 4194304 | tf_op jit(solution)/shard_map/all_to_all | solution.py:43
  237.5 2.5 copy.29
  240.0 2.7 %reshape_reshape.11 = f32[16,256,128]{2,1,0:T(8,128)} reshape(f32[16,32,1024]{2,1,0:T(8,128)} %copy.29) | data formatting | bytes 4194304 | tf_op jit(solution)/shard_map/reshape;reshape | solution.py:45
  242.7 4.1 %copy.30 = f32[16,256,128]{2,0,1:T(8,128)} copy(f32[16,256,128]{2,1,0:T(8,128)} %reshape_reshape.11) | data formatting | bytes 4194304 | tf_op jit(solution)/shard_map/reshape;reshape | solution.py:45
  246.9 2.2 gather_fusion.3
  249.1 0.1 broadcast_select_fusion
  249.2 2.7 %fusion.1 = f32[8,2,8,128]{3,2,1,0:T(8,128)S(1)} fusion(f32[16,8,6,128]{3,0,2,1:T(8,128)S(1)} %bitcast.83, f32[8,6,128,128]{3,2,1,0:T(8,128)S(1)} %copy-done), kind=kOutput, calls=%fused_computation.6 | convolution fusion | flops 151011328 | bytes 3604480 | tf_op jit(solution)/shard_map/rkij,trkj->tri/dot_general | solution.py:47
  251.9 0.0 copy-done.7
  251.9 0.6 bitcast_subtract_fusion
  (42 shorter events, 0.2 us)
Async XLA Ops:
  0.6 78.3 %copy-start = (f32[8,6,128,128]{3,2,1,0:T(8,128)S(1)}, f32[8,6,128,128]{3,2,1,0:T(8,128)}, u32[]{:S(2)}) copy-start(f32[8,6,128,128]{3,2,1,0:T(8,128)} %param.11) | copy-start | bytes 9437188
  3.2 11.4 %copy-start.18 = (s32[8,6]{1,0:T(8,128)S(1)}, s32[8,6]{1,0:T(8,128)}, u32[]{:S(2)}) copy-start(s32[8,6]{1,0:T(8,128)} %param.12) | copy-start | bytes 580
  3.2 62.5 %all-to-all-start = ((f32[32,16,1024]{2,1,0:T(8,128)}), f32[32,16,1024]{2,1,0:T(8,128)}, u32[]{:S(2)}, u32[]{:S(2)}) async-start(f32[32,16,1024]{2,1,0:T(8,128)} %stack.6), calls=%async_computation | async-start | bytes 4194304 | tf_op jit(solution)/shard_map/all_to_all | solution.py:43
  78.8 3.5 %copy-start.8 = (f32[16,1024]{1,0:T(8,128)S(1)}, f32[16,1024]{1,0:T(8,128)}, u32[]{:S(2)}) copy-start(f32[16,1024]{1,0:T(8,128)} %param.9) | copy-start | bytes 196612
  78.8 3.5 %copy-start.15 = (f32[16,1024]{1,0:T(8,128)S(1)}, f32[16,1024]{1,0:T(8,128)}, u32[]{:S(2)}) copy-start(f32[16,1024]{1,0:T(8,128)} %param.8) | copy-start | bytes 196612
  81.7 0.6 copy-start.1
  82.4 0.6 copy-start.11
  84.6 6.5 %copy-start.4 = (f32[16,1024]{1,0:T(8,128)S(1)}, f32[16,1024]{1,0:T(8,128)}, u32[]{:S(2)}) copy-start(f32[16,1024]{1,0:T(8,128)} %param.10) | copy-start | bytes 196612
  84.6 12.9 %copy-start.17 = (s32[3,1024]{1,0:T(4,128)S(1)}, s32[3,1024]{1,0:T(4,128)}, u32[]{:S(2)}) copy-start(s32[3,1024]{1,0:T(4,128)} %param.13) | copy-start | bytes 36868
  84.6 76.0 %all-to-all-start.1 = ((f32[32,16,1024]{2,1,0:T(8,128)}), f32[32,16,1024]{2,1,0:T(8,128)}, u32[]{:S(2)}, u32[]{:S(2)}) async-start(f32[32,16,1024]{2,1,0:T(8,128)} %stack.7), calls=%async_computation.1 | async-start | bytes 4194304 | tf_op jit(solution)/shard_map/all_to_all | solution.py:43
  91.1 44.0 %collective-permute-start = (f32[16,128]{1,0:T(8,128)S(1)}, f32[16,128]{1,0:T(8,128)S(1)}, u32[]{:S(2)}, u32[]{:S(2)}) collective-permute-start(f32[16,128]{1,0:T(8,128)S(1)} %get-tuple-element.8), channel_id=1, source_target_pairs={{0,16},{16,32},{32,48},{48,64},{64,80},{80,96},{96,112},{112,128},... | collective-permute-start | bytes 24584 | tf_op jit(solution)/shard_map/ppermute | solution.py:18
  95.5 42.9 %collective-permute-start.1 = (f32[16,128]{1,0:T(8,128)S(1)}, f32[16,128]{1,0:T(8,128)S(1)}, u32[]{:S(2)}, u32[]{:S(2)}) collective-permute-start(f32[16,128]{1,0:T(8,128)S(1)} %get-tuple-element.9), channel_id=1, source_target_pairs={{16,0},{32,16},{48,32},{64,48},{80,64},{96,80},{112,96},{128,112},... | collective-permute-start | bytes 24584 | tf_op jit(solution)/shard_map/ppermute | solution.py:21
  153.5 0.6 copy-start.13
  154.1 6.4 %collective-permute-start.2 = (f32[1,1024]{1,0:T(1,128)S(1)}, f32[1,1024]{1,0:T(1,128)S(1)}, u32[]{:S(2)}, u32[]{:S(2)}) collective-permute-start(f32[1,1024]{1,0:T(1,128)S(1)} %slice.39), channel_id=1, source_target_pairs={{0,1},{1,2},{2,3},{3,4},{4,5},{5,6},{6,7},{7,8},{8,9},{9,10},{10,1... | collective-permute-start | bytes 12296 | tf_op jit(solution)/shard_map/ppermute | solution.py:29
  173.7 2.9 %copy-start.2 = (f32[8,2,8,128]{3,2,1,0:T(8,128)S(1)}, f32[8,2,8,128]{3,2,1,0:T(8,128)}, u32[]{:S(2)}) copy-start(f32[8,2,8,128]{3,2,1,0:T(8,128)} %copy-done.1) | copy-start | bytes 196612
  173.7 2.9 %copy-start.5 = (f32[16,1024]{1,0:T(8,128)S(1)}, f32[16,1024]{1,0:T(8,128)}, u32[]{:S(2)}) copy-start(f32[16,1024]{1,0:T(8,128)} %param.10) | copy-start | bytes 196612
  173.7 2.9 %copy-start.9 = (f32[16,1024]{1,0:T(8,128)S(1)}, f32[16,1024]{1,0:T(8,128)}, u32[]{:S(2)}) copy-start(f32[16,1024]{1,0:T(8,128)} %param.9) | copy-start | bytes 196612
  173.8 2.9 %copy-start.12 = (f32[16,1024]{1,0:T(8,128)S(1)}, f32[16,1024]{1,0:T(8,128)}, u32[]{:S(2)}) copy-start(f32[16,1024]{1,0:T(8,128)} %copy-done.11) | copy-start | bytes 196612
  173.8 2.9 %copy-start.14 = (f32[16,1024]{1,0:T(8,128)S(1)}, f32[16,1024]{1,0:T(8,128)}, u32[]{:S(2)}) copy-start(f32[16,1024]{1,0:T(8,128)} %copy-done.13) | copy-start | bytes 196612
  176.6 60.8 %copy-start.6 = (f32[8,2,8,128]{3,2,1,0:T(8,128)}, f32[8,2,8,128]{3,2,1,0:T(8,128)S(1)}, u32[]{:S(2)}) copy-start(f32[8,2,8,128]{3,2,1,0:T(8,128)S(1)} %fusion.3) | copy-start | bytes 196612
  177.4 60.1 %copy-start.16 = (f32[16,1024]{1,0:T(8,128)}, f32[16,1024]{1,0:T(8,128)S(1)}, u32[]{:S(2)}) copy-start(f32[16,1024]{1,0:T(8,128)S(1)} %get-tuple-element.5) | copy-start | bytes 196612
  249.0 2.9 %copy-start.3 = (f32[8,2,8,128]{3,2,1,0:T(8,128)S(1)}, f32[8,2,8,128]{3,2,1,0:T(8,128)}, u32[]{:S(2)}) copy-start(f32[8,2,8,128]{3,2,1,0:T(8,128)} %copy-done.1) | copy-start | bytes 196612
  249.0 2.9 %copy-start.7 = (f32[8,2,8,128]{3,2,1,0:T(8,128)S(1)}, f32[8,2,8,128]{3,2,1,0:T(8,128)}, u32[]{:S(2)}) copy-start(f32[8,2,8,128]{3,2,1,0:T(8,128)} %copy-done.6) | copy-start | bytes 196612
  249.0 2.9 %copy-start.10 = (f32[16,1024]{1,0:T(8,128)S(1)}, f32[16,1024]{1,0:T(8,128)}, u32[]{:S(2)}) copy-start(f32[16,1024]{1,0:T(8,128)} %param.9) | copy-start | bytes 196612
